TPU v7x, 128 devices: a whole 4x4x4 slice. The times are simulated.
128 devices in a mesh: tok: 16 (over x, y), wid: 8 (over z, core).
Axes of the slice: x: 4, y: 4, z: 4, core: 2. Of those that a mesh axis runs over, the one named last changes fastest.
Arguments:
- patches: bfloat16 [1536, 8, 6144], P('tok', None, 'wid'), may hold values from -6 to 6
- w_query: bfloat16 [6144, 4096], P('tok', 'wid'), may hold values from -0.102062073 to 0.102062073
- w_key: bfloat16 [6144, 4096], P('tok', 'wid'), may hold values from -0.102062073 to 0.102062073
- w_value: bfloat16 [6144, 4096], P('tok', 'wid'), may hold values from -0.078125 to 0.078125
- q_gain: float32 [4096], P('wid'), may hold values from 0.5 to 6
- k_gain: float32 [4096], P('wid'), may hold values from 0.5 to 6
- w_out: bfloat16 [4096, 6144], P('tok', 'wid'), may hold values from -0.09375 to 0.09375
Outputs:
- layer_out: bfloat16 [1536, 8, 6144], P('tok', None, 'wid')
All inputs are finite; a program needn't handle non-finite values.
Results may differ from a plain program's by a relative error of at most 0.0034.
The roundings to bfloat16 on the way count: a program that leaves them out, or rounds other values in their place, can miss the bound.
Values may be sent and summed in bfloat16 or wider, within the bound.
No kernel may reach another device: no remote copies, remote signals or barrier semaphores. Data moves between devices by JAX's collectives and lax.ppermute only.
A program may use at most 128 MiB of HBM per device.

v0:
```python
import jax
import jax.numpy as jnp
from jax import lax
from jax.sharding import PartitionSpec as P

D = 6144
HEAD_DIM = 128
HD = 4096
RING = 4


def layer_norm_rows(values, eps):
    mean = jnp.mean(values, axis=-1, keepdims=True)
    var = jnp.mean(values * values, axis=-1, keepdims=True) - mean * mean
    return (values - mean) * lax.rsqrt(var + eps)


def add_rows(left, piece):
    return jnp.dot(left, piece, preferred_element_type=jnp.float32)


def head_norm(values, gain, eps):
    rows, images, width = values.shape
    heads_here = width // HEAD_DIM
    shaped = values.reshape(rows, images, heads_here, HEAD_DIM)
    normed = layer_norm_rows(shaped, eps) * gain.reshape(heads_here, HEAD_DIM)
    return normed.astype(jnp.bfloat16).reshape(rows, images * heads_here, HEAD_DIM)


def shift_pairs(sx, sy):
    return [
        (x * RING + y, ((x + sx) % RING) * RING + (y + sy) % RING)
        for x in range(RING)
        for y in range(RING)
    ]


def ring_step(group, along_x):
    sx, sy = (1, 0) if along_x else (0, 1)
    from_minus = lax.ppermute(group, "tok", shift_pairs(sx, sy))
    from_plus = lax.ppermute(group, "tok", shift_pairs(-sx, -sy))
    half = group.shape[-1] // 2
    first = lax.ppermute(from_minus[..., :half], "tok", shift_pairs(sx, sy))
    second = lax.ppermute(from_plus[..., half:], "tok", shift_pairs(-sx, -sy))
    across = jnp.concatenate([first, second], axis=-1)
    return [group, from_plus, across, from_minus]


def ring_gather(blocks):
    half = blocks.shape[-1] // 2
    parts = []
    for y_first, piece in ((True, blocks[..., :half]), (False, blocks[..., half:])):
        inner = jnp.stack(ring_step(piece, not y_first), axis=1)
        outer = jnp.stack(ring_step(inner, y_first), axis=1)
        if not y_first:
            outer = jnp.swapaxes(outer, 1, 2)
        parts.append(outer)
    whole = jnp.concatenate(parts, axis=-1)
    m, rows, cols = blocks.shape
    return whole.reshape(m, RING * RING * rows, cols)


def roll_blocks(values):
    t = lax.axis_index("tok")
    out = values
    for axis, shift in ((-3, t // RING), (-2, t % RING)):
        doubled = jnp.concatenate([out, out], axis=axis)
        starts = [0] * out.ndim
        starts[out.ndim + axis] = shift
        out = lax.dynamic_slice(doubled, starts, out.shape)
    return out


def local(patches, w_query, w_key, w_value, q_gain, k_gain, w_out):
    local_rows, images, local_width = patches.shape
    whole_raw = lax.all_gather(patches, "wid", axis=2, tiled=True)
    rolled = roll_blocks(whole_raw.reshape(local_rows, images, RING, RING, D // (RING * RING)))
    rolled = rolled.reshape(local_rows * images, D)
    flat = layer_norm_rows(rolled.astype(jnp.float32), 1e-06).astype(jnp.bfloat16)

    gathered = ring_gather(jnp.stack([w_query, w_key, w_value]))
    query = add_rows(flat, gathered[0])
    key = add_rows(flat, gathered[1])
    value = add_rows(flat, gathered[2])
    head_width = query.shape[1]
    heads_here = head_width // HEAD_DIM
    qnorm = head_norm(query.reshape(local_rows, images, head_width), q_gain, 1e-06)
    knorm = head_norm(key.reshape(local_rows, images, head_width), k_gain, 1e-06)
    vshaped = value.astype(jnp.bfloat16).reshape(local_rows, images * heads_here, HEAD_DIM)
    qfull, kfull, vfull = (
        lax.all_to_all(qnorm, "tok", split_axis=1, concat_axis=0, tiled=True),
        lax.all_to_all(knorm, "tok", split_axis=1, concat_axis=0, tiled=True),
        lax.all_to_all(vshaped, "tok", split_axis=1, concat_axis=0, tiled=True),
    )
    seq_rows, item_count, _ = qfull.shape
    block = min(512, seq_rows)
    blocks = qfull.reshape(seq_rows // block, block, item_count, HEAD_DIM)
    scale = HEAD_DIM ** (-0.5)

    def attend(qblock):
        scores = (
            jnp.einsum("qid,kid->iqk", qblock, kfull, preferred_element_type=jnp.float32) * scale
        )
        top = jnp.max(scores, axis=-1, keepdims=True)
        expo = jnp.exp(scores - top)
        probs = (expo / jnp.sum(expo, axis=-1, keepdims=True)).astype(jnp.bfloat16)
        return jnp.einsum("iqk,kid->qid", probs, vfull, preferred_element_type=jnp.float32).astype(
            jnp.bfloat16
        )

    attended = lax.map(attend, blocks).reshape(seq_rows, item_count, HEAD_DIM)
    returned = lax.all_to_all(attended, "tok", split_axis=0, concat_axis=1, tiled=True)
    mixed = returned.reshape(local_rows, images, head_width)
    mixed_whole = lax.all_gather(mixed, "wid", axis=2, tiled=True).reshape(local_rows * images, HD)
    branch = add_rows(mixed_whole, lax.all_gather(w_out, "tok", axis=0, tiled=True))
    as_float = patches.astype(jnp.float32)
    return (as_float + branch.reshape(local_rows, images, local_width)).astype(jnp.bfloat16)


def solution(mesh):
    placed = (
        P("tok", None, "wid"),
        P("tok", "wid"),
        P("tok", "wid"),
        P("tok", "wid"),
        P("wid"),
        P("wid"),
        P("tok", "wid"),
    )
    return jax.shard_map(
        local, mesh=mesh, in_specs=placed, out_specs=P("tok", None, "wid"), check_vma=False
    )
```

profile of v0, /device:TPU:1, one launch (start us, length us, event | category | flops | bytes accessed | tf_op | source)
XLA Modules:
  0.0 449.6 jit_solution(7976528101446662955)
XLA Ops:
  12.3 12.6 %collective-permute-done.9 = bf16[3,384,256]{2,1,0:T(8,128)(2,1)S(1)} collective-permute-done((bf16[3,384,256]{2,1,0:T(8,128)(2,1)S(1)}, bf16[3,384,256]{2,1,0:T(8,128)(2,1)S(1)}, u32[]{:S(2)}, u32[]{:S(2)}) %collective-permute-start.9) | collective-permute-done | bytes 589856 | tf_op jit(solution)/shard_map/ppermute | solution.py:40
  37.1 5.5 %collective-permute-done.1 = bf16[3,384,256]{2,1,0:T(8,128)(2,1)S(1)} collective-permute-done((bf16[3,384,256]{2,1,0:T(8,128)(2,1)S(1)}, bf16[3,384,256]{2,1,0:T(8,128)(2,1)S(1)}, u32[]{:S(2)}, u32[]{:S(2)}) %collective-permute-start.1) | collective-permute-done | bytes 589856 | tf_op jit(solution)/shard_map/ppermute | solution.py:40
  45.5 53.8 %collective-permute-done.2 = bf16[3,384,128]{2,1,0:T(8,128)(2,1)S(1)} collective-permute-done((bf16[3,384,128]{2,1,0:T(8,128)(2,1)S(1)}, bf16[3,384,128]{2,1,0:T(8,128)(2,1)S(1)}, u32[]{:S(2)}, u32[]{:S(2)}) %collective-permute-start.2) | collective-permute-done | bytes 294944 | tf_op jit(solution)/shard_map/ppermute | solution.py:43
  111.7 55.5 %collective-permute-done.5 = bf16[3,4,384,256]{3,2,0,1:T(8,128)(2,1)} collective-permute-done((bf16[3,4,384,256]{3,2,0,1:T(8,128)(2,1)}, bf16[3,4,384,256]{3,2,0,1:T(8,128)(2,1)}, u32[]{:S(2)}, u32[]{:S(2)}) %collective-permute-start.5) | collective-permute-done | bytes 2359328 | tf_op jit(solution)/shard_map/ppermute | solution.py:40
  176.7 33.1 %collective-permute-done.6 = bf16[3,4,384,128]{3,2,0,1:T(8,128)(2,1)S(1)} collective-permute-done((bf16[3,4,384,128]{3,2,0,1:T(8,128)(2,1)S(1)}, bf16[3,4,384,128]{3,2,0,1:T(8,128)(2,1)S(1)}, u32[]{:S(2)}, u32[]{:S(2)}) %collective-permute-start.6) | collective-permute-done | bytes 1179680 | tf_op jit(solution)/shard_map/ppermute | solution.py:43
  210.2 10.1 %pad_maximum_fusion.1 = (bf16[1,4,4,384,512]{4,3,2,1,0:T(8,128)(2,1)}, bf16[1,4,4,384,512]{4,3,2,1,0:T(8,128)(2,1)}, bf16[1,4,4,384,512]{4,3,2,1,0:T(8,128)(2,1)}) fusion(bf16[3,4,4,384,256]{4,3,2,1,0:T(8,128)(2,1)S(1)} %maximum_bitcast_fusion, bf16[3,1,4,384,256]{4,3,0,2,1:T(8,128)(2,1)} %bitcast.17, ...), kind=kLoop, calls=%fused_computation.39 | loop fusion | flops 51904512 | bytes 37748736 | tf_op jit(solution)/shard_map/concatenate | solution.py:58
  220.4 8.6 %copy.109 = bf16[512,6144]{1,0:T(8,128)(2,1)} copy(bf16[512,6144]{0,1:T(8,128)(2,1)} %bitcast.128) | data formatting | bytes 12582912 | tf_op jit(solution)/shard_map/dot_general | solution.py:19
  229.0 8.7 %copy.102 = bf16[512,6144]{1,0:T(8,128)(2,1)} copy(bf16[512,6144]{0,1:T(8,128)(2,1)} %bitcast.127) | data formatting | bytes 12582912 | tf_op jit(solution)/shard_map/dot_general | solution.py:19
  237.7 7.1 %fusion.31 = bf16[96,8,4,4,384]{4,1,3,2,0:T(8,128)(2,1)S(1)} fusion(s32[]{:T(128)S(6)} %select_n.18, bf16[96,8,4,4,384]{4,1,3,2,0:T(8,128)(2,1)} %bitcast.132), kind=kLoop, calls=%fused_computation.34 | loop fusion | flops 4718592 | bytes 18874372 | tf_op jit(solution)/shard_map/concatenate | solution.py:67
  244.7 8.8 %convert_reduce_fusion = (f32[96,8]{1,0:T(8,128)S(1)}, f32[96,8]{1,0:T(8,128)S(1)}, bf16[96,8,4,4,384]{4,1,3,2,0:T(8,128)(2,1)}) fusion(s32[]{:T(128)S(6)} %select_n.20, bf16[96,8,4,4,384]{4,1,3,2,0:T(8,128)(2,1)S(1)} %fusion.31), kind=kLoop, calls=%fused_computation.21 | loop fusion | flops 23591424 | bytes 18880516 | tf_op jit(solution)/shard_map/reduce_sum | solution.py:13
  253.9 12.5 %fusion.28 = bf16[96,8,4,4,384]{4,1,3,2,0:T(8,128)(2,1)} fusion(bf16[96,8,4,4,384]{4,1,3,2,0:T(8,128)(2,1)} %get-tuple-element.74, f32[96,8]{1,0:T(8,128)S(1)} %copy.94, f32[96,8]{1,0:T(8,128)S(1)} %copy.92), kind=kLoop, calls=%fused_computation.27 | loop fusion | flops 18874368 | bytes 18880512 | tf_op jit(solution)/shard_map/convert_element_type | solution.py:79
  266.4 9.9 %convolution_convert_fusion = bf16[768,512]{1,0:T(8,128)(2,1)S(1)} fusion(bf16[768,6144]{1,0:T(8,128)(2,1)} %bitcast.129, bf16[6144,512]{1,0:T(8,128)(2,1)} %bitcast.133), kind=kOutput, calls=%fused_computation.51 | convolution fusion | flops 4832231424 | bytes 16515072 | tf_op jit(solution)/shard_map/dot_general | solution.py:19
  278.0 5.8 %all-to-all-start.2 = ((bf16[96,32,128]{2,0,1:T(8,128)(2,1)}), bf16[96,32,128]{2,0,1:T(8,128)(2,1)S(1)}, u32[]{:S(2)}, u32[]{:S(2)}) async-start(bf16[96,32,128]{2,0,1:T(8,128)(2,1)} %copy.116), calls=%async_computation.2 | async-start | bytes 1572864 | tf_op jit(solution)/shard_map/all_to_all | solution.py:93
  283.9 9.8 %fusion.40 = (f32[96,8,4]{1,2,0:T(4,128)S(1)}, f32[96,8,4]{1,2,0:T(4,128)S(1)}, f32[96,8,4,128]{3,1,2,0:T(8,128)S(1)}) fusion(bf16[96,8,6144,1]{2,1,3,0:T(8,128)(2,1)} %bitcast.130, bf16[4,128,6144,1]{2,1,0,3:T(8,128)(2,1)} %bitcast.135), kind=kOutput, calls=%fused_computation.65 | convolution fusion | flops 4833011712 | bytes 17326080 | tf_op jit(solution)/shard_map/dot_general | solution.py:19
  296.3 6.7 %all-to-all-start.1 = ((bf16[96,32,128]{2,0,1:T(8,128)(2,1)}), bf16[96,32,128]{2,0,1:T(8,128)(2,1)S(1)}, u32[]{:S(2)}, u32[]{:S(2)}) async-start(bf16[96,32,128]{2,0,1:T(8,128)(2,1)} %bitcast.49), calls=%async_computation.1 | async-start | bytes 1572864 | tf_op jit(solution)/shard_map/all_to_all | solution.py:92
  303.1 9.9 %fusion.41 = (f32[96,8,4]{1,2,0:T(4,128)S(1)}, f32[96,8,4]{1,2,0:T(4,128)S(1)}, f32[96,8,4,128]{3,1,2,0:T(8,128)S(1)}) fusion(bf16[96,8,6144,1]{2,1,3,0:T(8,128)(2,1)} %bitcast.131, bf16[4,128,6144,1]{2,1,0,3:T(8,128)(2,1)} %bitcast.134), kind=kOutput, calls=%fused_computation.66 | convolution fusion | flops 4833011712 | bytes 17326080 | tf_op jit(solution)/shard_map/dot_general | solution.py:19
  317.6 6.7 %all-to-all-start = ((bf16[96,32,128]{2,0,1:T(8,128)(2,1)}), bf16[96,32,128]{2,0,1:T(8,128)(2,1)S(1)}, u32[]{:S(2)}, u32[]{:S(2)}) async-start(bf16[96,32,128]{2,0,1:T(8,128)(2,1)} %bitcast.38), calls=%async_computation | async-start | bytes 1572864 | tf_op jit(solution)/shard_map/all_to_all | solution.py:91
  324.5 10.3 %all-to-all-done = bf16[96,32,128]{2,0,1:T(8,128)(2,1)S(1)} async-done(((bf16[96,32,128]{2,0,1:T(8,128)(2,1)}), bf16[96,32,128]{2,0,1:T(8,128)(2,1)S(1)}, u32[]{:S(2)}, u32[]{:S(2)}) %all-to-all-start) | async-done | bytes 786464 | tf_op jit(solution)/shard_map/all_to_all | solution.py:91
  334.8 27.6 %while.10 = (s32[]{:T(128)}, bf16[3,512,2,128]{3,1,0,2:T(8,128)(2,1)}, bf16[3,512,2,128]{3,1,0,2:T(8,128)(2,1)S(1)}, bf16[1536,2,128]{2,0,1:T(8,128)(2,1)S(1)}, bf16[1536,2,128]{2,0,1:T(8,128)(2,1)S(1)}, /*index=5*/s32[]{:T(128)}) while((s32[]{:T(128)}, bf16[3,512,2,128]{3,1,0,2:T(8,128)(2,1)}, bf16[3,512,2,128]{3,1,0,2:T(8,128)(2,1)S(1)}, ...), condition=%wide.region_9.10_spmd, body=%wide.region_6.9_spmd.sunk | while | flops 813303296 | bytes 14688841 | solution.py:111
  335.1 4.6 %fusion.67 = (f32[2,512]{1,0:T(2,128)S(1)}, f32[2,512,1536]{2,1,0:T(8,128)}) fusion(bf16[1536,2,128]{2,0,1:T(8,128)(2,1)S(1)} %get-tuple-element.146, bf16[3,512,2,128]{3,1,0,2:T(8,128)(2,1)S(1)} %get-tuple-element.145, s32[]{:T(128)} %get-tuple-element.137), kind=kOutput, calls=%fused_computation.67.clone.1 | convolution fusion | flops 407373312 | bytes 7344132 | tf_op jit(solution)/shard_map/while/body/eval_jaxpr/sub | solution.py:105
  362.5 6.8 %copy.120 = bf16[1536,2,128]{2,1,0:T(2,128)(2,1)S(1)} copy(bf16[1536,2,128]{2,0,1:T(8,128)(2,1)} %bitcast.149) | data formatting | bytes 1572864 | tf_op jit(solution)/shard_map/reshape | solution.py:111
  369.3 13.1 %all_to_all.66 = bf16[1536,2,128]{2,1,0:T(2,128)(2,1)S(1)} all-to-all(bf16[1536,2,128]{2,1,0:T(2,128)(2,1)S(1)} %copy.120), channel_id=1, replica_groups=mesh['tok'=16,'wid'=8] {'tok'}, dimensions={0} | all-to-all | bytes 1572864 | tf_op jit(solution)/shard_map/all_to_all | solution.py:112
  384.6 48.3 %all-gather.6.cloned.1.call-done = bf16[96,8,4096]{2,1,0:T(8,128)(2,1)} async-done(((bf16[96,8,512]{2,1,0:T(8,128)(2,1)}), bf16[96,8,4096]{2,1,0:T(8,128)(2,1)}) %all-gather.6.cloned.1.call-update) | async-done | bytes 6291472 | tf_op jit(solution)/shard_map/all_gather | solution.py:114
  432.8 9.8 %add_convert_fusion = bf16[96,8,768]{2,1,0:T(8,128)(2,1)} fusion(bf16[96,8,768]{2,1,0:T(8,128)(2,1)S(1)} %copy-done.5, bf16[96,8,4096]{2,1,0:T(8,128)(2,1)} %all-gather.6.cloned.1.call-done, bf16[4096,768]{1,0:T(8,128)(2,1)} %all-gather.8.cloned.1.call-done), kind=kOutput, calls=%fused_computation.46 | convolution fusion | flops 4833607680 | bytes 14942208 | tf_op jit(solution)/shard_map/dot_general | solution.py:19
  (101 shorter events, 77.3 us)
Async XLA Ops:
  6.5 231.1 %all-gather.4.cloned.1.call-start = ((), (), s32[]{:S(2)}) async-start(), calls=%async_computation.4 | async-start | bytes 10616832 | tf_op jit(solution)/shard_map/all_gather | solution.py:76
  7.3 377.3 %all-gather.8.cloned.1.call-start = ((), (), s32[]{:S(2)}) async-start(), calls=%async_computation.6 | async-start | bytes 6684672 | tf_op jit(solution)/shard_map/all_gather | solution.py:115
  8.9 16.0 %collective-permute-start.9 = (bf16[3,384,256]{2,1,0:T(8,128)(2,1)S(1)}, bf16[3,384,256]{2,1,0:T(8,128)(2,1)S(1)}, u32[]{:S(2)}, u32[]{:S(2)}) collective-permute-start(bf16[3,384,256]{2,1,0:T(8,128)(2,1)S(1)} %get-tuple-element.86), channel_id=1, source_target_pairs={{0,32},{8,40},{16,48},{24,56},{32,64},{40,72},{48,80},{56,88},{64,... | collective-permute-start | bytes 1769480 | tf_op jit(solution)/shard_map/ppermute | solution.py:40
  11.0 14.3 %collective-permute-start.8 = (bf16[3,384,256]{2,1,0:T(8,128)(2,1)S(1)}, bf16[3,384,256]{2,1,0:T(8,128)(2,1)S(1)}, u32[]{:S(2)}, u32[]{:S(2)}) collective-permute-start(bf16[3,384,256]{2,1,0:T(8,128)(2,1)S(1)} %get-tuple-element.86), channel_id=1, source_target_pairs={{0,96},{8,104},{16,112},{24,120},{32,0},{40,8},{48,16},{56,24},{64... | collective-permute-start | bytes 1769480 | tf_op jit(solution)/shard_map/ppermute | solution.py:41
  25.0 8.3 %collective-permute-start.10 = (bf16[3,384,128]{2,1,0:T(8,128)(2,1)S(1)}, bf16[3,384,128]{2,1,0:T(8,128)(2,1)S(1)}, u32[]{:S(2)}, u32[]{:S(2)}) collective-permute-start(bf16[3,384,128]{2,1,0:T(8,128)(2,1)S(1)} %slice.61), channel_id=1, source_target_pairs={{0,32},{8,40},{16,48},{24,56},{32,64},{40,72},{48,80},{56,88},{64,... | collective-permute-start | bytes 884744 | tf_op jit(solution)/shard_map/ppermute | solution.py:43
  25.4 7.9 %collective-permute-start.11 = (bf16[3,384,128]{2,1,0:T(8,128)(2,1)S(1)}, bf16[3,384,128]{2,1,0:T(8,128)(2,1)S(1)}, u32[]{:S(2)}, u32[]{:S(2)}) collective-permute-start(bf16[3,384,128]{2,1,0:T(8,128)(2,1)S(1)} %slice.62), channel_id=1, source_target_pairs={{0,96},{8,104},{16,112},{24,120},{32,0},{40,8},{48,16},{56,24},{64... | collective-permute-start | bytes 884744 | tf_op jit(solution)/shard_map/ppermute | solution.py:44
  27.8 14.7 %collective-permute-start.1 = (bf16[3,384,256]{2,1,0:T(8,128)(2,1)S(1)}, bf16[3,384,256]{2,1,0:T(8,128)(2,1)S(1)}, u32[]{:S(2)}, u32[]{:S(2)}) collective-permute-start(bf16[3,384,256]{2,1,0:T(8,128)(2,1)S(1)} %get-tuple-element.87), channel_id=1, source_target_pairs={{0,8},{8,16},{16,24},{24,0},{32,40},{40,48},{48,56},{56,32},{64,72... | collective-permute-start | bytes 1769480 | tf_op jit(solution)/shard_map/ppermute | solution.py:40
  29.4 13.3 %collective-permute-start = (bf16[3,384,256]{2,1,0:T(8,128)(2,1)S(1)}, bf16[3,384,256]{2,1,0:T(8,128)(2,1)S(1)}, u32[]{:S(2)}, u32[]{:S(2)}) collective-permute-start(bf16[3,384,256]{2,1,0:T(8,128)(2,1)S(1)} %get-tuple-element.87), channel_id=1, source_target_pairs={{0,24},{8,0},{16,8},{24,16},{32,56},{40,32},{48,40},{56,48},{64,88... | collective-permute-start | bytes 1769480 | tf_op jit(solution)/shard_map/ppermute | solution.py:41
  33.8 70.6 %collective-permute-start.13 = (bf16[3,4,384,256]{3,2,1,0:T(8,128)(2,1)S(1)}, bf16[3,4,384,256]{3,2,1,0:T(8,128)(2,1)S(1)}, u32[]{:S(2)}, u32[]{:S(2)}) collective-permute-start(bf16[3,4,384,256]{3,2,1,0:T(8,128)(2,1)S(1)} %get-tuple-element.81), channel_id=1, source_target_pairs={{0,8},{8,16},{16,24},{24,0},{32,40},{40,48},{48,56},{56,32},{64,72... | collective-permute-start | bytes 7077896 | tf_op jit(solution)/shard_map/ppermute | solution.py:40
  35.5 71.5 %collective-permute-start.12 = (bf16[3,4,384,256]{3,2,1,0:T(8,128)(2,1)S(1)}, bf16[3,4,384,256]{3,2,1,0:T(8,128)(2,1)S(1)}, u32[]{:S(2)}, u32[]{:S(2)}) collective-permute-start(bf16[3,4,384,256]{3,2,1,0:T(8,128)(2,1)S(1)} %get-tuple-element.81), channel_id=1, source_target_pairs={{0,24},{8,0},{16,8},{24,16},{32,56},{40,32},{48,40},{56,48},{64,88... | collective-permute-start | bytes 7077896 | tf_op jit(solution)/shard_map/ppermute | solution.py:41
  42.6 56.7 %collective-permute-start.2 = (bf16[3,384,128]{2,1,0:T(8,128)(2,1)S(1)}, bf16[3,384,128]{2,1,0:T(8,128)(2,1)S(1)}, u32[]{:S(2)}, u32[]{:S(2)}) collective-permute-start(bf16[3,384,128]{2,1,0:T(8,128)(2,1)S(1)} %slice.56), channel_id=1, source_target_pairs={{0,8},{8,16},{16,24},{24,0},{32,40},{40,48},{48,56},{56,32},{64,72... | collective-permute-start | bytes 884744 | tf_op jit(solution)/shard_map/ppermute | solution.py:43
  42.8 56.6 %collective-permute-start.3 = (bf16[3,384,128]{2,1,0:T(8,128)(2,1)S(1)}, bf16[3,384,128]{2,1,0:T(8,128)(2,1)S(1)}, u32[]{:S(2)}, u32[]{:S(2)}) collective-permute-start(bf16[3,384,128]{2,1,0:T(8,128)(2,1)S(1)} %slice.57), channel_id=1, source_target_pairs={{0,24},{8,0},{16,8},{24,16},{32,56},{40,32},{48,40},{56,48},{64,88... | collective-permute-start | bytes 884744 | tf_op jit(solution)/shard_map/ppermute | solution.py:44
  101.8 65.5 %collective-permute-start.5 = (bf16[3,4,384,256]{3,2,0,1:T(8,128)(2,1)}, bf16[3,4,384,256]{3,2,0,1:T(8,128)(2,1)}, u32[]{:S(2)}, u32[]{:S(2)}) collective-permute-start(bf16[3,4,384,256]{3,2,0,1:T(8,128)(2,1)} %get-tuple-element.83), channel_id=1, source_target_pairs={{0,32},{8,40},{16,48},{24,56},{32,64},{40,72},{48,80},{56,88},{64,... | collective-permute-start | bytes 7077896 | tf_op jit(solution)/shard_map/ppermute | solution.py:40
  101.8 66.9 %collective-permute-start.4 = (bf16[3,4,384,256]{3,2,0,1:T(8,128)(2,1)}, bf16[3,4,384,256]{3,2,0,1:T(8,128)(2,1)}, u32[]{:S(2)}, u32[]{:S(2)}) collective-permute-start(bf16[3,4,384,256]{3,2,0,1:T(8,128)(2,1)} %get-tuple-element.83), channel_id=1, source_target_pairs={{0,96},{8,104},{16,112},{24,120},{32,0},{40,8},{48,16},{56,24},{64... | collective-permute-start | bytes 7077896 | tf_op jit(solution)/shard_map/ppermute | solution.py:41
  106.2 67.2 %collective-permute-start.14 = (bf16[3,4,384,128]{3,2,1,0:T(8,128)(2,1)S(1)}, bf16[3,4,384,128]{3,2,1,0:T(8,128)(2,1)}, u32[]{:S(2)}, u32[]{:S(2)}) collective-permute-start(bf16[3,4,384,128]{3,2,1,0:T(8,128)(2,1)S(1)} %slice.63), channel_id=1, source_target_pairs={{0,8},{8,16},{16,24},{24,0},{32,40},{40,48},{48,56},{56,32},{64,72... | collective-permute-start | bytes 3538952 | tf_op jit(solution)/shard_map/ppermute | solution.py:43
  109.7 63.6 %collective-permute-start.15 = (bf16[3,4,384,128]{3,2,1,0:T(8,128)(2,1)}, bf16[3,4,384,128]{3,2,1,0:T(8,128)(2,1)}, u32[]{:S(2)}, u32[]{:S(2)}) collective-permute-start(bf16[3,4,384,128]{3,2,1,0:T(8,128)(2,1)} %slice.64), channel_id=1, source_target_pairs={{0,24},{8,0},{16,8},{24,16},{32,56},{40,32},{48,40},{56,48},{64,88... | collective-permute-start | bytes 3538952 | tf_op jit(solution)/shard_map/ppermute | solution.py:44
  111.7 63.6 %copy-start.2 = (bf16[3,4,384,256]{3,2,1,0:T(8,128)(2,1)S(1)}, bf16[3,4,384,256]{3,2,1,0:T(8,128)(2,1)}, u32[]{:S(2)}) copy-start(bf16[3,4,384,256]{3,2,1,0:T(8,128)(2,1)} %copy-done.1) | copy-start | bytes 7077892
  168.6 41.3 %collective-permute-start.6 = (bf16[3,4,384,128]{3,2,0,1:T(8,128)(2,1)S(1)}, bf16[3,4,384,128]{3,2,0,1:T(8,128)(2,1)S(1)}, u32[]{:S(2)}, u32[]{:S(2)}) collective-permute-start(bf16[3,4,384,128]{3,2,0,1:T(8,128)(2,1)S(1)} %slice.58), channel_id=1, source_target_pairs={{0,32},{8,40},{16,48},{24,56},{32,64},{40,72},{48,80},{56,88},{64,... | collective-permute-start | bytes 3538952 | tf_op jit(solution)/shard_map/ppermute | solution.py:43
  170.1 39.8 %collective-permute-start.7 = (bf16[3,4,384,128]{3,2,0,1:T(8,128)(2,1)S(1)}, bf16[3,4,384,128]{3,2,0,1:T(8,128)(2,1)S(1)}, u32[]{:S(2)}, u32[]{:S(2)}) collective-permute-start(bf16[3,4,384,128]{3,2,0,1:T(8,128)(2,1)S(1)} %slice.59), channel_id=1, source_target_pairs={{0,96},{8,104},{16,112},{24,120},{32,0},{40,8},{48,16},{56,24},{64... | collective-permute-start | bytes 3538952 | tf_op jit(solution)/shard_map/ppermute | solution.py:44
  278.0 18.3 %all-to-all-start.2 = ((bf16[96,32,128]{2,0,1:T(8,128)(2,1)}), bf16[96,32,128]{2,0,1:T(8,128)(2,1)S(1)}, u32[]{:S(2)}, u32[]{:S(2)}) async-start(bf16[96,32,128]{2,0,1:T(8,128)(2,1)} %copy.116), calls=%async_computation.2 | async-start | bytes 1572864 | tf_op jit(solution)/shard_map/all_to_all | solution.py:93
  296.3 21.3 %all-to-all-start.1 = ((bf16[96,32,128]{2,0,1:T(8,128)(2,1)}), bf16[96,32,128]{2,0,1:T(8,128)(2,1)S(1)}, u32[]{:S(2)}, u32[]{:S(2)}) async-start(bf16[96,32,128]{2,0,1:T(8,128)(2,1)} %bitcast.49), calls=%async_computation.1 | async-start | bytes 1572864 | tf_op jit(solution)/shard_map/all_to_all | solution.py:92
  317.6 17.1 %all-to-all-start = ((bf16[96,32,128]{2,0,1:T(8,128)(2,1)}), bf16[96,32,128]{2,0,1:T(8,128)(2,1)S(1)}, u32[]{:S(2)}, u32[]{:S(2)}) async-start(bf16[96,32,128]{2,0,1:T(8,128)(2,1)} %bitcast.38), calls=%async_computation | async-start | bytes 1572864 | tf_op jit(solution)/shard_map/all_to_all | solution.py:91
  324.3 108.5 %all-gather.6.cloned.1.call-start = ((), (), s32[]{:S(2)}) async-start(), calls=%async_computation.5 | async-start | bytes 7077888 | tf_op jit(solution)/shard_map/all_gather | solution.py:114
  362.5 70.4 %copy-start.5 = (bf16[96,8,768]{2,1,0:T(8,128)(2,1)S(1)}, bf16[96,8,768]{2,1,0:T(8,128)(2,1)}, u32[]{:S(2)}) copy-start(bf16[96,8,768]{2,1,0:T(8,128)(2,1)} %param.9) | copy-start | bytes 3538948
  (5 other events, 110.4 us)
Sparse Core Ops, SparseCore 0:
  9.0 57.8 all-gather.3
  111.8 87.1 all-gather.7
  384.7 48.1 all-gather.5
where the time goes:
time: 457 us; the launch traced here: 450 us
  waiting for transfers between devices  222 us (49%)
  matrix products  66.7 us (15%)
  other arithmetic  49.8 us (11%)
  starting transfers between devices  43.4 us (9%)
  local copies, waits for them, and re-layouts  40 us (9%)
  between operations  14 us (3%)
  blocking collectives  13.1 us (3%)
    ppermute x4, waiting for transfers between devices, ring_step(): first = lax.ppermute(from_minus[..., :half], 'tok', shift_pairs(sx, sy))  89.4 us
    ppermute x4, waiting for transfers between devices, ring_step(): from_minus = lax.ppermute(group, 'tok', shift_pairs(sx, sy))  73.6 us
    all_gather x1, waiting for transfers between devices, local(): lax.all_gather(mixed, 'wid', axis=2, tiled=True)  48.3 us
    dot_general x4, matrix products, add_rows(): return jnp.dot(left, piece, preferred_element_type=jnp.float32)  39.3 us
    dot_general x2, local copies, waits for them, and re-layouts, add_rows(): return jnp.dot(left, piece, preferred_element_type=jnp.float32)  17.3 us
    sub x3, matrix products, attend(): expo = jnp.exp(scores - top)  13.8 us
    dot_general x3, matrix products, attend(): jnp.einsum('iqk,kid->qid', probs, vfull, preferred_element_type=jnp.float32)  13.5 us
    all_to_all x1, blocking collectives, local(): lax.all_to_all(attended, 'tok', split_axis=0, concat_axis=1, tiled=True)  13.1 us
  transfers between devices with their start and end apart: 22, of which 8 were waited for; matrix products, arithmetic and copies ran while one was open for 32% of the time, Pallas kernels for 0%

commit v1 on v0

--- a/solution.py
+++ b/solution.py
@@ -60,28 +60,39 @@
     return whole.reshape(m, RING * RING * rows, cols)
 
 
-def roll_blocks(values):
+def roll_major(values):
     t = lax.axis_index("tok")
     out = values
-    for axis, shift in ((-3, t // RING), (-2, t % RING)):
+    for axis, shift in ((0, t // RING), (1, t % RING)):
         doubled = jnp.concatenate([out, out], axis=axis)
         starts = [0] * out.ndim
-        starts[out.ndim + axis] = shift
+        starts[axis] = shift
         out = lax.dynamic_slice(doubled, starts, out.shape)
     return out
 
 
+def contract_blocks(blocks, weight):
+    rows = blocks.shape[-1]
+    shaped = weight.reshape(RING, RING, rows, weight.shape[-1])
+    return jnp.einsum("abtr,abrc->tc", blocks, shaped, preferred_element_type=jnp.float32)
+
+
 def local(patches, w_query, w_key, w_value, q_gain, k_gain, w_out):
     local_rows, images, local_width = patches.shape
-    whole_raw = lax.all_gather(patches, "wid", axis=2, tiled=True)
-    rolled = roll_blocks(whole_raw.reshape(local_rows, images, RING, RING, D // (RING * RING)))
-    rolled = rolled.reshape(local_rows * images, D)
-    flat = layer_norm_rows(rolled.astype(jnp.float32), 1e-06).astype(jnp.bfloat16)
+    tokens = local_rows * images
+    sub = D // (RING * RING)
+    pieces = patches.reshape(tokens, local_width // sub, sub).transpose(1, 0, 2)
+    whole_raw = lax.all_gather(pieces, "wid", axis=0, tiled=True).astype(jnp.float32)
+    mean = jnp.mean(whole_raw, axis=(0, 2), keepdims=True)
+    var = jnp.mean(whole_raw * whole_raw, axis=(0, 2), keepdims=True) - mean * mean
+    normed = ((whole_raw - mean) * lax.rsqrt(var + 1e-06)).astype(jnp.bfloat16)
+    normed = normed.reshape(RING, RING, tokens, sub)
+    rolled = roll_major(normed)
 
-    gathered = ring_gather(jnp.stack([w_query, w_key, w_value]))
-    query = add_rows(flat, gathered[0])
-    key = add_rows(flat, gathered[1])
-    value = add_rows(flat, gathered[2])
+    gathered = ring_gather(jnp.stack([w_query, w_key]))
+    query = contract_blocks(rolled, gathered[0])
+    key = contract_blocks(rolled, gathered[1])
+    value = contract_blocks(normed, lax.all_gather(w_value, "tok", axis=0, tiled=True))
     head_width = query.shape[1]
     heads_here = head_width // HEAD_DIM
     qnorm = head_norm(query.reshape(local_rows, images, head_width), q_gain, 1e-06)
@@ -111,7 +122,7 @@
     attended = lax.map(attend, blocks).reshape(seq_rows, item_count, HEAD_DIM)
     returned = lax.all_to_all(attended, "tok", split_axis=0, concat_axis=1, tiled=True)
     mixed = returned.reshape(local_rows, images, head_width)
-    mixed_whole = lax.all_gather(mixed, "wid", axis=2, tiled=True).reshape(local_rows * images, HD)
+    mixed_whole = lax.all_gather(mixed, "wid", axis=2, tiled=True).reshape(tokens, HD)
     branch = add_rows(mixed_whole, lax.all_gather(w_out, "tok", axis=0, tiled=True))
     as_float = patches.astype(jnp.float32)
     return (as_float + branch.reshape(local_rows, images, local_width)).astype(jnp.bfloat16)

time: 457 us -> 382 us (0.84)
  waiting for transfers between devices: 222 us -> 166 us
  local copies, waits for them, and re-layouts: 40 us -> 26.7 us
  other arithmetic: 49.8 us -> 44.6 us
    ppermute x4, waiting for transfers between devices: 89.4 us -> 57.3 us  [ring_step(): first = lax.ppermute(from_minus[..., :half], 'tok', shift_pairs(sx, sy))]
    dot_general x4 -> x1, matrix products: 39.3 us -> 9.78 us  [add_rows(): return jnp.dot(left, piece, preferred_element_type=jnp.float32)]
    dot_general x0 -> x3, matrix products: none -> 29.5 us  [contract_blocks(): jnp.einsum('abtr,abrc->tc', blocks, shaped, preferred_element_type=jnp.fl...]
    ppermute x4, waiting for transfers between devices: 73.6 us -> 50 us  [ring_step(): from_minus = lax.ppermute(group, 'tok', shift_pairs(sx, sy))]
    dot_general x2 -> x0, local copies, waits for them, and re-layouts: 17.3 us -> none  [add_rows(): return jnp.dot(left, piece, preferred_element_type=jnp.float32)]
    all_to_all x1, waiting for transfers between devices: 10.3 us -> 0.01 us  [local(): lax.all_to_all(qnorm, 'tok', split_axis=1, concat_axis=0, tiled=True)]
    all_to_all x1, waiting for transfers between devices: 0.01 us -> 10 us  [local(): lax.all_to_all(vshaped, 'tok', split_axis=1, concat_axis=0, tiled=True)]
    all_gather x2 -> x3, waiting for transfers between devices: 48.3 us -> 47.5 us  [the longest x1 47.4 us: local(): lax.all_gather(mixed, 'wid', axis=2, tiled=True).reshape(tokens, HD)]
  transfers between devices with their start and end apart: 22 -> 23, of which waited for: 8 -> 8; matrix products, arithmetic and copies ran while one was open for 32% -> 32% of each run, Pallas kernels for 0% -> 0%
where the time goes in v1:
time: 382 us; the launch traced here: 375 us
  waiting for transfers between devices  166 us (43%)
  matrix products  66.7 us (17%)
  other arithmetic  44.6 us (12%)
  starting transfers between devices  43.7 us (11%)
  local copies, waits for them, and re-layouts  26.7 us (7%)
  between operations  14 us (4%)
  blocking collectives  13.2 us (3%)
    ppermute x4, waiting for transfers between devices, ring_step(): first = lax.ppermute(from_minus[..., :half], 'tok', shift_pairs(sx, sy))  57.3 us
    ppermute x4, waiting for transfers between devices, ring_step(): from_minus = lax.ppermute(group, 'tok', shift_pairs(sx, sy))  50 us
    all_gather x1, waiting for transfers between devices, local(): lax.all_gather(mixed, 'wid', axis=2, tiled=True).reshape(tokens, HD)  47.4 us
    dot_general x3, matrix products, contract_blocks(): jnp.einsum('abtr,abrc->tc', blocks, shaped, preferred_element_type=jnp.fl...  29.5 us
    sub x3, matrix products, attend(): expo = jnp.exp(scores - top)  13.8 us
    dot_general x3, matrix products, attend(): jnp.einsum('iqk,kid->qid', probs, vfull, preferred_element_type=jnp.float32)  13.5 us
    all_to_all x1, blocking collectives, local(): lax.all_to_all(attended, 'tok', split_axis=0, concat_axis=1, tiled=True)  13.2 us
    concatenate x1, other arithmetic, roll_major(): doubled = jnp.concatenate([out, out], axis=axis)  10.9 us
  transfers between devices with their start and end apart: 23, of which 8 were waited for; matrix products, arithmetic and copies ran while one was open for 32% of the time, Pallas kernels for 0%

profile of v1, /device:TPU:1, one launch (start us, length us, event | category | flops | bytes accessed | tf_op | source)
XLA Modules:
  0.0 374.5 jit_solution(2092163565706268601)
XLA Ops:
  15.4 8.4 %collective-permute-done.9 = bf16[2,384,256]{1,2,0:T(8,128)(2,1)S(1)} collective-permute-done((bf16[2,384,256]{1,2,0:T(8,128)(2,1)S(1)}, bf16[2,384,256]{1,2,0:T(8,128)(2,1)S(1)}, u32[]{:S(2)}, u32[]{:S(2)}) %collective-permute-start.9) | collective-permute-done | bytes 393248 | tf_op jit(solution)/shard_map/ppermute | solution.py:40
  40.0 34.9 %collective-permute-done.2 = bf16[2,384,128]{1,2,0:T(8,128)(2,1)S(1)} collective-permute-done((bf16[2,384,128]{1,2,0:T(8,128)(2,1)S(1)}, bf16[2,384,128]{1,2,0:T(8,128)(2,1)S(1)}, u32[]{:S(2)}, u32[]{:S(2)}) %collective-permute-start.2) | collective-permute-done | bytes 196640 | tf_op jit(solution)/shard_map/ppermute | solution.py:43
  85.0 38.2 %collective-permute-done.5 = bf16[2,4,384,256]{2,3,0,1:T(8,128)(2,1)S(1)} collective-permute-done((bf16[2,4,384,256]{2,3,0,1:T(8,128)(2,1)S(1)}, bf16[2,4,384,256]{2,3,0,1:T(8,128)(2,1)S(1)}, u32[]{:S(2)}, u32[]{:S(2)}) %collective-permute-start.5) | collective-permute-done | bytes 1572896 | tf_op jit(solution)/shard_map/ppermute | solution.py:40
  136.1 22.0 %collective-permute-done.6 = bf16[2,4,384,128]{2,3,0,1:T(8,128)(2,1)} collective-permute-done((bf16[2,4,384,128]{2,3,0,1:T(8,128)(2,1)}, bf16[2,4,384,128]{2,3,0,1:T(8,128)(2,1)}, u32[]{:S(2)}, u32[]{:S(2)}) %collective-permute-start.6) | collective-permute-done | bytes 786464 | tf_op jit(solution)/shard_map/ppermute | solution.py:43
  159.7 6.2 %pad_maximum_fusion = (bf16[1,4,4,384,512]{3,4,2,1,0:T(8,128)(2,1)}, bf16[1,4,4,384,512]{3,4,2,1,0:T(8,128)(2,1)}) fusion(bf16[2,4,4,384,256]{3,4,2,1,0:T(8,128)(2,1)S(1)} %maximum_bitcast_fusion, bf16[2,1,4,384,256]{3,4,0,2,1:T(8,128)(2,1)S(1)} %bitcast.165, bf16[2,1,4,384,256]{3,4,0,2,1:T(8,128)(2,1)S(1)} %maximum_bitcast_fusion.1, ...), kind=kLoop, calls=%fused_computation.39 | loop fusion | flops 34603008 | bytes 25165824 | tf_op jit(solution)/shard_map/concatenate | solution.py:58
  165.9 7.0 %convert_reduce_fusion = (f32[768]{0:T(1024)S(1)}, f32[768]{0:T(1024)S(1)}) fusion(bf16[16,768,384]{2,1,0:T(8,128)(2,1)} %all-gather.5.cloned.1.call-done), kind=kLoop, calls=%fused_computation.21 | loop fusion | flops 18872832 | bytes 9443328 | tf_op jit(solution)/shard_map/reduce_sum | solution.py:86
  172.9 10.0 %fusion.28 = bf16[16,768,384]{2,1,0:T(8,128)(2,1)} fusion(bf16[16,768,384]{2,1,0:T(8,128)(2,1)} %all-gather.5.cloned.1.call-done, f32[768]{0:T(1024)S(1)} %get-tuple-element.90, f32[768]{0:T(1024)S(1)} %get-tuple-element.89), kind=kLoop, calls=%fused_computation.23 | loop fusion | flops 18874368 | bytes 18880512 | tf_op jit(solution)/shard_map/convert_element_type | solution.py:88
  182.9 10.9 %fusion.32 = bf16[4,4,768,384]{3,2,1,0:T(8,128)(2,1)} fusion(s32[]{:T(128)S(6)} %select_n.18, bf16[4,4,768,384]{3,2,1,0:T(8,128)(2,1)} %bitcast.158), kind=kLoop, calls=%fused_computation.33 | loop fusion | flops 4718592 | bytes 18874372 | tf_op jit(solution)/shard_map/concatenate | solution.py:67
  193.8 10.1 %bitcast_reduce_fusion = (f32[96,8,4]{1,2,0:T(4,128)S(1)}, f32[96,8,4,128,1,1]{3,1,5,2,0,4:T(8,128)S(1)}) fusion(bf16[4,128,4,4,384,1]{4,1,0,3,2,5:T(8,128)(2,1)} %bitcast.161, s32[]{:T(128)S(6)} %select_n.20, bf16[4,4,768,384]{3,2,1,0:T(8,128)(2,1)} %fusion.32), kind=kOutput, calls=%fused_computation.52 | convolution fusion | flops 4836946944 | bytes 17313796 | tf_op jit(solution)/shard_map/abtr,abrc->tc/dot_general | solution.py:77
  206.9 6.2 %all-to-all-start.1 = ((bf16[96,32,128]{2,0,1:T(8,128)(2,1)}), bf16[96,32,128]{2,0,1:T(8,128)(2,1)S(1)}, u32[]{:S(2)}, u32[]{:S(2)}) async-start(bf16[96,32,128]{2,0,1:T(8,128)(2,1)} %bitcast.53), calls=%async_computation.1 | async-start | bytes 1572864 | tf_op jit(solution)/shard_map/all_to_all | solution.py:103
  213.1 10.0 %bitcast_reduce_fusion.1 = (f32[96,8,4]{1,2,0:T(4,128)S(1)}, f32[96,8,4,128,1,1]{3,1,5,2,0,4:T(8,128)S(1)}) fusion(bf16[4,128,4,4,384,1]{4,1,0,3,2,5:T(8,128)(2,1)} %bitcast.160, s32[]{:T(128)S(6)} %select_n.20, bf16[4,4,768,384]{3,2,1,0:T(8,128)(2,1)} %fusion.32), kind=kOutput, calls=%fused_computation.59 | convolution fusion | flops 4836946944 | bytes 17313796 | tf_op jit(solution)/shard_map/abtr,abrc->tc/dot_general | solution.py:77
  226.1 6.4 %all-to-all-start = ((bf16[96,32,128]{2,0,1:T(8,128)(2,1)}), bf16[96,32,128]{2,0,1:T(8,128)(2,1)S(1)}, u32[]{:S(2)}, u32[]{:S(2)}) async-start(bf16[96,32,128]{2,0,1:T(8,128)(2,1)} %bitcast.40), calls=%async_computation | async-start | bytes 1572864 | tf_op jit(solution)/shard_map/all_to_all | solution.py:102
  232.6 9.5 %bitcast_convert_fusion = bf16[768,512]{1,0:T(8,128)(2,1)S(1)} fusion(bf16[4,4,768,384]{3,2,1,0:T(8,128)(2,1)} %bitcast.159, bf16[4,4,384,512]{3,2,1,0:T(8,128)(2,1)} %bitcast.185), kind=kOutput, calls=%fused_computation.51 | convolution fusion | flops 4832231424 | bytes 16515072 | tf_op jit(solution)/shard_map/abtr,abrc->tc/dot_general | solution.py:77
  243.7 6.7 %all-to-all-start.2 = ((bf16[96,32,128]{2,0,1:T(8,128)(2,1)}), bf16[96,32,128]{2,0,1:T(8,128)(2,1)S(1)}, u32[]{:S(2)}, u32[]{:S(2)}) async-start(bf16[96,32,128]{2,0,1:T(8,128)(2,1)} %copy.164), calls=%async_computation.2 | async-start | bytes 1572864 | tf_op jit(solution)/shard_map/all_to_all | solution.py:104
  250.8 10.0 %all-to-all-done.2 = bf16[96,32,128]{2,0,1:T(8,128)(2,1)S(1)} async-done(((bf16[96,32,128]{2,0,1:T(8,128)(2,1)}), bf16[96,32,128]{2,0,1:T(8,128)(2,1)S(1)}, u32[]{:S(2)}, u32[]{:S(2)}) %all-to-all-start.2) | async-done | bytes 786464 | tf_op jit(solution)/shard_map/all_to_all | solution.py:104
  260.9 27.3 %while.10 = (s32[]{:T(128)}, bf16[3,512,2,128]{3,1,0,2:T(8,128)(2,1)}, bf16[3,512,2,128]{3,1,0,2:T(8,128)(2,1)S(1)}, bf16[1536,2,128]{2,0,1:T(8,128)(2,1)S(1)}, bf16[1536,2,128]{2,0,1:T(8,128)(2,1)S(1)}, /*index=5*/s32[]{:T(128)}) while((s32[]{:T(128)}, bf16[3,512,2,128]{3,1,0,2:T(8,128)(2,1)}, bf16[3,512,2,128]{3,1,0,2:T(8,128)(2,1)S(1)}, ...), condition=%wide.region_9.10_spmd, body=%wide.region_6.9_spmd.sunk | while | flops 813303296 | bytes 14688841 | solution.py:122
  260.9 4.6 %fusion.79 = (f32[2,512]{1,0:T(2,128)S(1)}, f32[2,512,1536]{2,1,0:T(8,128)}) fusion(bf16[1536,2,128]{2,0,1:T(8,128)(2,1)S(1)} %get-tuple-element.145, bf16[3,512,2,128]{3,1,0,2:T(8,128)(2,1)S(1)} %get-tuple-element.144, s32[]{:T(128)} %get-tuple-element.136), kind=kOutput, calls=%fused_computation.80.clone.1 | convolution fusion | flops 407373312 | bytes 7344132 | tf_op jit(solution)/shard_map/while/body/eval_jaxpr/sub | solution.py:116
  265.5 4.5 %fusion.80 = bf16[3,512,2,128]{3,1,0,2:T(8,128)(2,1)} fusion(bf16[3,512,2,128]{3,1,0,2:T(8,128)(2,1)} %get-tuple-element.137, s32[]{:T(128)} %get-tuple-element.136, bf16[1536,2,128]{2,0,1:T(8,128)(2,1)S(1)} %get-tuple-element.146, f32[2,512,1536]{2,1,0:T(8,128)} %get-tuple-element.128, f32[2,512]{1,0:T(2,128)S(1)} %get-tuple-element.129), kind=kOutput, calls=%fused_computation.9.clone.1 | convolution fusion | flops 405929984 | bytes 7344640 | tf_op jit(solution)/shard_map/while/body/eval_jaxpr/iqk,kid->qid/dot_general | solution.py:118
  270.0 4.6 %fusion.79 = (f32[2,512]{1,0:T(2,128)S(1)}, f32[2,512,1536]{2,1,0:T(8,128)}) fusion(bf16[1536,2,128]{2,0,1:T(8,128)(2,1)S(1)} %get-tuple-element.145, bf16[3,512,2,128]{3,1,0,2:T(8,128)(2,1)S(1)} %get-tuple-element.144, s32[]{:T(128)} %get-tuple-element.136), kind=kOutput, calls=%fused_computation.80.clone.1 | convolution fusion | flops 407373312 | bytes 7344132 | tf_op jit(solution)/shard_map/while/body/eval_jaxpr/sub | solution.py:116
  279.1 4.6 %fusion.79 = (f32[2,512]{1,0:T(2,128)S(1)}, f32[2,512,1536]{2,1,0:T(8,128)}) fusion(bf16[1536,2,128]{2,0,1:T(8,128)(2,1)S(1)} %get-tuple-element.145, bf16[3,512,2,128]{3,1,0,2:T(8,128)(2,1)S(1)} %get-tuple-element.144, s32[]{:T(128)} %get-tuple-element.136), kind=kOutput, calls=%fused_computation.80.clone.1 | convolution fusion | flops 407373312 | bytes 7344132 | tf_op jit(solution)/shard_map/while/body/eval_jaxpr/sub | solution.py:116
  288.2 6.8 %copy.168 = bf16[1536,2,128]{2,1,0:T(2,128)(2,1)S(1)} copy(bf16[1536,2,128]{2,0,1:T(8,128)(2,1)} %bitcast.182) | data formatting | bytes 1572864 | tf_op jit(solution)/shard_map/reshape | solution.py:122
  295.0 13.2 %all_to_all.66 = bf16[1536,2,128]{2,1,0:T(2,128)(2,1)S(1)} all-to-all(bf16[1536,2,128]{2,1,0:T(2,128)(2,1)S(1)} %copy.168), channel_id=1, replica_groups=mesh['tok'=16,'wid'=8] {'tok'}, dimensions={0} | all-to-all | bytes 1572864 | tf_op jit(solution)/shard_map/all_to_all | solution.py:123
  310.3 47.4 %all-gather.9.cloned.1.call-done = bf16[96,8,4096]{2,1,0:T(8,128)(2,1)} async-done(((bf16[96,8,512]{2,1,0:T(8,128)(2,1)}), bf16[96,8,4096]{2,1,0:T(8,128)(2,1)}) %all-gather.9.cloned.1.call-update) | async-done | bytes 6291472 | tf_op jit(solution)/shard_map/all_gather | solution.py:125
  357.8 9.8 %add_convert_fusion = bf16[96,8,768]{2,1,0:T(8,128)(2,1)} fusion(bf16[96,8,768]{2,1,0:T(8,128)(2,1)S(1)} %copy-done.6, bf16[96,8,4096]{2,1,0:T(8,128)(2,1)} %all-gather.9.cloned.1.call-done, bf16[4096,768]{1,0:T(8,128)(2,1)} %all-gather.11.cloned.1.call-done), kind=kOutput, calls=%fused_computation.46 | convolution fusion | flops 4833607680 | bytes 14942208 | tf_op jit(solution)/shard_map/dot_general | solution.py:19
  (111 shorter events, 68.6 us)
Async XLA Ops:
  6.5 159.4 %all-gather.5.cloned.1.call-start = ((), (), s32[]{:S(2)}) async-start(), calls=%async_computation.4 | async-start | bytes 10616832 | tf_op jit(solution)/shard_map/all_gather | solution.py:85
  10.6 222.0 %all-gather.7.cloned.1.call-start = ((), (), s32[]{:S(2)}) async-start(), calls=%async_computation.5 | async-start | bytes 6684672 | tf_op jit(solution)/shard_map/all_gather | solution.py:95
  11.3 299.0 %all-gather.11.cloned.1.call-start = ((), (), s32[]{:S(2)}) async-start(), calls=%async_computation.7 | async-start | bytes 6684672 | tf_op jit(solution)/shard_map/all_gather | solution.py:126
  11.9 11.8 %collective-permute-start.9 = (bf16[2,384,256]{1,2,0:T(8,128)(2,1)S(1)}, bf16[2,384,256]{1,2,0:T(8,128)(2,1)S(1)}, u32[]{:S(2)}, u32[]{:S(2)}) collective-permute-start(bf16[2,384,256]{1,2,0:T(8,128)(2,1)S(1)} %get-tuple-element.83), channel_id=1, source_target_pairs={{0,32},{8,40},{16,48},{24,56},{32,64},{40,72},{48,80},{56,88},{64,... | collective-permute-start | bytes 1179656 | tf_op jit(solution)/shard_map/ppermute | solution.py:40
  14.0 10.1 %collective-permute-start.8 = (bf16[2,384,256]{1,2,0:T(8,128)(2,1)S(1)}, bf16[2,384,256]{1,2,0:T(8,128)(2,1)S(1)}, u32[]{:S(2)}, u32[]{:S(2)}) collective-permute-start(bf16[2,384,256]{1,2,0:T(8,128)(2,1)S(1)} %get-tuple-element.83), channel_id=1, source_target_pairs={{0,96},{8,104},{16,112},{24,120},{32,0},{40,8},{48,16},{56,24},{64... | collective-permute-start | bytes 1179656 | tf_op jit(solution)/shard_map/ppermute | solution.py:41
  23.8 6.2 %collective-permute-start.10 = (bf16[2,384,128]{1,2,0:T(8,128)(2,1)S(1)}, bf16[2,384,128]{1,2,0:T(8,128)(2,1)S(1)}, u32[]{:S(2)}, u32[]{:S(2)}) collective-permute-start(bf16[2,384,128]{1,2,0:T(8,128)(2,1)S(1)} %slice.56), channel_id=1, source_target_pairs={{0,32},{8,40},{16,48},{24,56},{32,64},{40,72},{48,80},{56,88},{64,... | collective-permute-start | bytes 589832 | tf_op jit(solution)/shard_map/ppermute | solution.py:43
  24.2 5.9 %collective-permute-start.11 = (bf16[2,384,128]{1,2,0:T(8,128)(2,1)S(1)}, bf16[2,384,128]{1,2,0:T(8,128)(2,1)S(1)}, u32[]{:S(2)}, u32[]{:S(2)}) collective-permute-start(bf16[2,384,128]{1,2,0:T(8,128)(2,1)S(1)} %slice.57), channel_id=1, source_target_pairs={{0,96},{8,104},{16,112},{24,120},{32,0},{40,8},{48,16},{56,24},{64... | collective-permute-start | bytes 589832 | tf_op jit(solution)/shard_map/ppermute | solution.py:44
  26.6 10.5 %collective-permute-start.1 = (bf16[2,384,256]{1,2,0:T(8,128)(2,1)S(1)}, bf16[2,384,256]{1,2,0:T(8,128)(2,1)S(1)}, u32[]{:S(2)}, u32[]{:S(2)}) collective-permute-start(bf16[2,384,256]{1,2,0:T(8,128)(2,1)S(1)} %get-tuple-element.84), channel_id=1, source_target_pairs={{0,8},{8,16},{16,24},{24,0},{32,40},{40,48},{48,56},{56,32},{64,72... | collective-permute-start | bytes 1179656 | tf_op jit(solution)/shard_map/ppermute | solution.py:40
  28.2 9.0 %collective-permute-start = (bf16[2,384,256]{1,2,0:T(8,128)(2,1)S(1)}, bf16[2,384,256]{1,2,0:T(8,128)(2,1)S(1)}, u32[]{:S(2)}, u32[]{:S(2)}) collective-permute-start(bf16[2,384,256]{1,2,0:T(8,128)(2,1)S(1)} %get-tuple-element.84), channel_id=1, source_target_pairs={{0,24},{8,0},{16,8},{24,16},{32,56},{40,32},{48,40},{56,48},{64,88... | collective-permute-start | bytes 1179656 | tf_op jit(solution)/shard_map/ppermute | solution.py:41
  30.4 47.7 %collective-permute-start.13 = (bf16[2,4,384,256]{2,3,1,0:T(8,128)(2,1)S(1)}, bf16[2,4,384,256]{2,3,1,0:T(8,128)(2,1)S(1)}, u32[]{:S(2)}, u32[]{:S(2)}) collective-permute-start(bf16[2,4,384,256]{2,3,1,0:T(8,128)(2,1)S(1)} %get-tuple-element.80), channel_id=1, source_target_pairs={{0,8},{8,16},{16,24},{24,0},{32,40},{40,48},{48,56},{56,32},{64,72... | collective-permute-start | bytes 4718600 | tf_op jit(solution)/shard_map/ppermute | solution.py:40
  32.1 48.9 %collective-permute-start.12 = (bf16[2,4,384,256]{2,3,1,0:T(8,128)(2,1)S(1)}, bf16[2,4,384,256]{2,3,1,0:T(8,128)(2,1)S(1)}, u32[]{:S(2)}, u32[]{:S(2)}) collective-permute-start(bf16[2,4,384,256]{2,3,1,0:T(8,128)(2,1)S(1)} %get-tuple-element.80), channel_id=1, source_target_pairs={{0,24},{8,0},{16,8},{24,16},{32,56},{40,32},{48,40},{56,48},{64,88... | collective-permute-start | bytes 4718600 | tf_op jit(solution)/shard_map/ppermute | solution.py:41
  37.1 37.8 %collective-permute-start.2 = (bf16[2,384,128]{1,2,0:T(8,128)(2,1)S(1)}, bf16[2,384,128]{1,2,0:T(8,128)(2,1)S(1)}, u32[]{:S(2)}, u32[]{:S(2)}) collective-permute-start(bf16[2,384,128]{1,2,0:T(8,128)(2,1)S(1)} %slice.52), channel_id=1, source_target_pairs={{0,8},{8,16},{16,24},{24,0},{32,40},{40,48},{48,56},{56,32},{64,72... | collective-permute-start | bytes 589832 | tf_op jit(solution)/shard_map/ppermute | solution.py:43
  37.3 37.7 %collective-permute-start.3 = (bf16[2,384,128]{1,2,0:T(8,128)(2,1)S(1)}, bf16[2,384,128]{1,2,0:T(8,128)(2,1)S(1)}, u32[]{:S(2)}, u32[]{:S(2)}) collective-permute-start(bf16[2,384,128]{1,2,0:T(8,128)(2,1)S(1)} %slice.53), channel_id=1, source_target_pairs={{0,24},{8,0},{16,8},{24,16},{32,56},{40,32},{48,40},{56,48},{64,88... | collective-permute-start | bytes 589832 | tf_op jit(solution)/shard_map/ppermute | solution.py:44
  75.3 47.9 %collective-permute-start.5 = (bf16[2,4,384,256]{2,3,0,1:T(8,128)(2,1)S(1)}, bf16[2,4,384,256]{2,3,0,1:T(8,128)(2,1)S(1)}, u32[]{:S(2)}, u32[]{:S(2)}) collective-permute-start(bf16[2,4,384,256]{2,3,0,1:T(8,128)(2,1)S(1)} %get-tuple-element.82), channel_id=1, source_target_pairs={{0,32},{8,40},{16,48},{24,56},{32,64},{40,72},{48,80},{56,88},{64,... | collective-permute-start | bytes 4718600 | tf_op jit(solution)/shard_map/ppermute | solution.py:40
  75.4 49.9 %collective-permute-start.4 = (bf16[2,4,384,256]{2,3,0,1:T(8,128)(2,1)S(1)}, bf16[2,4,384,256]{2,3,0,1:T(8,128)(2,1)S(1)}, u32[]{:S(2)}, u32[]{:S(2)}) collective-permute-start(bf16[2,4,384,256]{2,3,0,1:T(8,128)(2,1)S(1)} %get-tuple-element.82), channel_id=1, source_target_pairs={{0,96},{8,104},{16,112},{24,120},{32,0},{40,8},{48,16},{56,24},{64... | collective-permute-start | bytes 4718600 | tf_op jit(solution)/shard_map/ppermute | solution.py:41
  80.2 50.7 %collective-permute-start.14 = (bf16[2,4,384,128]{2,3,1,0:T(8,128)(2,1)}, bf16[2,4,384,128]{2,3,1,0:T(8,128)(2,1)}, u32[]{:S(2)}, u32[]{:S(2)}) collective-permute-start(bf16[2,4,384,128]{2,3,1,0:T(8,128)(2,1)} %slice.58), channel_id=1, source_target_pairs={{0,8},{8,16},{16,24},{24,0},{32,40},{40,48},{48,56},{56,32},{64,72... | collective-permute-start | bytes 2359304 | tf_op jit(solution)/shard_map/ppermute | solution.py:43
  83.1 47.8 %collective-permute-start.15 = (bf16[2,4,384,128]{2,3,1,0:T(8,128)(2,1)}, bf16[2,4,384,128]{2,3,1,0:T(8,128)(2,1)}, u32[]{:S(2)}, u32[]{:S(2)}) collective-permute-start(bf16[2,4,384,128]{2,3,1,0:T(8,128)(2,1)} %slice.59), channel_id=1, source_target_pairs={{0,24},{8,0},{16,8},{24,16},{32,56},{40,32},{48,40},{56,48},{64,88... | collective-permute-start | bytes 2359304 | tf_op jit(solution)/shard_map/ppermute | solution.py:44
  125.3 32.8 %collective-permute-start.6 = (bf16[2,4,384,128]{2,3,0,1:T(8,128)(2,1)}, bf16[2,4,384,128]{2,3,0,1:T(8,128)(2,1)}, u32[]{:S(2)}, u32[]{:S(2)}) collective-permute-start(bf16[2,4,384,128]{2,3,0,1:T(8,128)(2,1)} %slice.54), channel_id=1, source_target_pairs={{0,32},{8,40},{16,48},{24,56},{32,64},{40,72},{48,80},{56,88},{64,... | collective-permute-start | bytes 2359304 | tf_op jit(solution)/shard_map/ppermute | solution.py:43
  127.5 30.6 %collective-permute-start.7 = (bf16[2,4,384,128]{2,3,0,1:T(8,128)(2,1)}, bf16[2,4,384,128]{2,3,0,1:T(8,128)(2,1)}, u32[]{:S(2)}, u32[]{:S(2)}) collective-permute-start(bf16[2,4,384,128]{2,3,0,1:T(8,128)(2,1)} %slice.55), channel_id=1, source_target_pairs={{0,96},{8,104},{16,112},{24,120},{32,0},{40,8},{48,16},{56,24},{64... | collective-permute-start | bytes 2359304 | tf_op jit(solution)/shard_map/ppermute | solution.py:44
  206.9 19.2 %all-to-all-start.1 = ((bf16[96,32,128]{2,0,1:T(8,128)(2,1)}), bf16[96,32,128]{2,0,1:T(8,128)(2,1)S(1)}, u32[]{:S(2)}, u32[]{:S(2)}) async-start(bf16[96,32,128]{2,0,1:T(8,128)(2,1)} %bitcast.53), calls=%async_computation.1 | async-start | bytes 1572864 | tf_op jit(solution)/shard_map/all_to_all | solution.py:103
  226.1 17.6 %all-to-all-start = ((bf16[96,32,128]{2,0,1:T(8,128)(2,1)}), bf16[96,32,128]{2,0,1:T(8,128)(2,1)S(1)}, u32[]{:S(2)}, u32[]{:S(2)}) async-start(bf16[96,32,128]{2,0,1:T(8,128)(2,1)} %bitcast.40), calls=%async_computation | async-start | bytes 1572864 | tf_op jit(solution)/shard_map/all_to_all | solution.py:102
  243.7 17.1 %all-to-all-start.2 = ((bf16[96,32,128]{2,0,1:T(8,128)(2,1)}), bf16[96,32,128]{2,0,1:T(8,128)(2,1)S(1)}, u32[]{:S(2)}, u32[]{:S(2)}) async-start(bf16[96,32,128]{2,0,1:T(8,128)(2,1)} %copy.164), calls=%async_computation.2 | async-start | bytes 1572864 | tf_op jit(solution)/shard_map/all_to_all | solution.py:104
  250.4 107.4 %all-gather.9.cloned.1.call-start = ((), (), s32[]{:S(2)}) async-start(), calls=%async_computation.6 | async-start | bytes 7077888 | tf_op jit(solution)/shard_map/all_gather | solution.py:125
  288.2 69.6 %copy-start.6 = (bf16[96,8,768]{2,1,0:T(8,128)(2,1)S(1)}, bf16[96,8,768]{2,1,0:T(8,128)(2,1)}, u32[]{:S(2)}) copy-start(bf16[96,8,768]{2,1,0:T(8,128)(2,1)} %param.9) | copy-start | bytes 3538948
  (10 other events, 91.0 us)
Sparse Core Ops, SparseCore 0:
  10.7 57.8 all-gather.4
  70.8 84.6 all-gather.6
  157.7 60.9 all-gather.10
  310.4 47.3 all-gather.8

commit v2 on v1

--- a/solution.py
+++ b/solution.py
@@ -2,6 +2,7 @@
 import jax.numpy as jnp
 from jax import lax
 from jax.sharding import PartitionSpec as P
+
 
 D = 6144
 HEAD_DIM = 128
@@ -98,13 +99,11 @@
     qnorm = head_norm(query.reshape(local_rows, images, head_width), q_gain, 1e-06)
     knorm = head_norm(key.reshape(local_rows, images, head_width), k_gain, 1e-06)
     vshaped = value.astype(jnp.bfloat16).reshape(local_rows, images * heads_here, HEAD_DIM)
-    qfull, kfull, vfull = (
-        lax.all_to_all(qnorm, "tok", split_axis=1, concat_axis=0, tiled=True),
-        lax.all_to_all(knorm, "tok", split_axis=1, concat_axis=0, tiled=True),
-        lax.all_to_all(vshaped, "tok", split_axis=1, concat_axis=0, tiled=True),
-    )
+    stacked = jnp.stack([qnorm, knorm, vshaped], axis=1)
+    spread = lax.all_to_all(stacked, "tok", split_axis=2, concat_axis=0, tiled=True)
+    qfull, kfull, vfull = spread[:, 0], spread[:, 1], spread[:, 2]
     seq_rows, item_count, _ = qfull.shape
-    block = min(512, seq_rows)
+    block = seq_rows
     blocks = qfull.reshape(seq_rows // block, block, item_count, HEAD_DIM)
     scale = HEAD_DIM ** (-0.5)
 
@@ -138,6 +137,7 @@
         P("wid"),
         P("tok", "wid"),
     )
+
     return jax.shard_map(
         local, mesh=mesh, in_specs=placed, out_specs=P("tok", None, "wid"), check_vma=False
     )

time: 382 us -> 364 us (0.953)
  blocking collectives: 13.2 us -> 47.1 us
  starting transfers between devices: 43.7 us -> 24.3 us
  matrix products: 66.7 us -> 53.8 us
  waiting for transfers between devices: 166 us -> 154 us
  local copies, waits for them, and re-layouts: 26.7 us -> 18.5 us
    all_to_all x0 -> x1, blocking collectives: none -> 32.9 us  [local(): lax.all_to_all(stacked, 'tok', split_axis=2, concat_axis=0, tiled=True)]
    all_to_all x3 -> x0, starting transfers between devices: 19.3 us -> none  [the longest x1 6.65 us: local(): lax.all_to_all(vshaped, 'tok', split_axis=1, concat_axis=0, tiled=True)]
    all_to_all x3 -> x0, waiting for transfers between devices: 10 us -> none  [the longest x1 10 us: local(): lax.all_to_all(vshaped, 'tok', split_axis=1, concat_axis=0, tiled=True)]
    reshape x3 -> x0, local copies, waits for them, and re-layouts: 8.48 us -> none  [the longest x1 6.8 us: local(): attended = lax.map(attend, blocks).reshape(seq_rows, item_count, HEAD_DIM)]
    sub x3 -> x1, matrix products: 13.8 us -> 5.81 us  [attend(): expo = jnp.exp(scores - top)]
    dot_general x3 -> x1, matrix products: 13.5 us -> 8.35 us  [attend(): jnp.einsum('iqk,kid->qid', probs, vfull, preferred_element_type=jnp.float32)]
  transfers between devices with their start and end apart: 23 -> 20, of which waited for: 8 -> 7; matrix products, arithmetic and copies ran while one was open for 32% -> 28% of each run, Pallas kernels for 0% -> 0%
where the time goes in v2:
time: 364 us; the launch traced here: 357 us
  waiting for transfers between devices  154 us (42%)
  matrix products  53.8 us (15%)
  blocking collectives  47.1 us (13%)
  other arithmetic  45.1 us (12%)
  starting transfers between devices  24.3 us (7%)
  local copies, waits for them, and re-layouts  18.5 us (5%)
  between operations  14.1 us (4%)
    ppermute x4, waiting for transfers between devices, ring_step(): first = lax.ppermute(from_minus[..., :half], 'tok', shift_pairs(sx, sy))  57.3 us
    ppermute x4, waiting for transfers between devices, ring_step(): from_minus = lax.ppermute(group, 'tok', shift_pairs(sx, sy))  50 us
    all_gather x1, waiting for transfers between devices, local(): lax.all_gather(mixed, 'wid', axis=2, tiled=True).reshape(tokens, HD)  45.7 us
    all_to_all x1, blocking collectives, local(): lax.all_to_all(stacked, 'tok', split_axis=2, concat_axis=0, tiled=True)  32.9 us
    dot_general x3, matrix products, contract_blocks(): jnp.einsum('abtr,abrc->tc', blocks, shaped, preferred_element_type=jnp.fl...  29.9 us
    all_to_all x1, blocking collectives, local(): lax.all_to_all(attended, 'tok', split_axis=0, concat_axis=1, tiled=True)  14.2 us
    concatenate x1, other arithmetic, roll_major(): doubled = jnp.concatenate([out, out], axis=axis)  10.8 us
    ppermute x4, starting transfers between devices, ring_step(): second = lax.ppermute(from_plus[..., half:], 'tok', shift_pairs(-sx, -sy))  10.5 us
  transfers between devices with their start and end apart: 20, of which 7 were waited for; matrix products, arithmetic and copies ran while one was open for 28% of the time, Pallas kernels for 0%

profile of v2, /device:TPU:1, one launch (start us, length us, event | category | flops | bytes accessed | tf_op | source)
XLA Modules:
  0.0 356.6 jit_solution(15697557287818177789)
XLA Ops:
  6.5 2.9 reshape.87
  15.4 8.4 %collective-permute-done.9 = bf16[2,384,256]{1,2,0:T(8,128)(2,1)S(1)} collective-permute-done((bf16[2,384,256]{1,2,0:T(8,128)(2,1)S(1)}, bf16[2,384,256]{1,2,0:T(8,128)(2,1)S(1)}, u32[]{:S(2)}, u32[]{:S(2)}) %collective-permute-start.9) | collective-permute-done | bytes 393248 | tf_op jit(solution)/shard_map/ppermute | solution.py:41
  24.2 2.5 collective-permute-start.11
  33.6 3.5 collective-permute-done.1
  37.3 2.7 collective-permute-start.3
  40.0 34.9 %collective-permute-done.2 = bf16[2,384,128]{1,2,0:T(8,128)(2,1)S(1)} collective-permute-done((bf16[2,384,128]{1,2,0:T(8,128)(2,1)S(1)}, bf16[2,384,128]{1,2,0:T(8,128)(2,1)S(1)}, u32[]{:S(2)}, u32[]{:S(2)}) %collective-permute-start.2) | collective-permute-done | bytes 196640 | tf_op jit(solution)/shard_map/ppermute | solution.py:44
  75.4 2.7 collective-permute-start.4
  85.0 38.1 %collective-permute-done.5 = bf16[2,4,384,256]{2,3,0,1:T(8,128)(2,1)S(1)} collective-permute-done((bf16[2,4,384,256]{2,3,0,1:T(8,128)(2,1)S(1)}, bf16[2,4,384,256]{2,3,0,1:T(8,128)(2,1)S(1)}, u32[]{:S(2)}, u32[]{:S(2)}) %collective-permute-start.5) | collective-permute-done | bytes 1572896 | tf_op jit(solution)/shard_map/ppermute | solution.py:41
  127.5 3.4 collective-permute-start.7
  132.6 3.6 %maximum_bitcast_fusion = bf16[2,4,4,384,256]{3,4,2,1,0:T(8,128)(2,1)S(1)} fusion(bf16[2,1,4,384,256]{3,4,1,2,0:T(8,128)(2,1)} %bitcast.154, bf16[2,1,4,384,256]{3,4,1,2,0:T(8,128)(2,1)S(1)} %maximum_bitcast_fusion.2, bf16[2,1,4,384,256]{3,4,1,2,0:T(8,128)(2,1)} %bitcast.155, bf16[2,1,4,384,256]{3,4,1,2,0:T(8,128)(2,1)S(1)} %get-tuple-element.26), kind=kLoop, calls=%fused_computation.29 | loop fusion | flops 9437184 | bytes 12582912 | tf_op jit(solution)/shard_map/transpose | solution.py:57
  136.2 21.9 %collective-permute-done.6 = bf16[2,4,384,128]{2,3,0,1:T(8,128)(2,1)} collective-permute-done((bf16[2,4,384,128]{2,3,0,1:T(8,128)(2,1)}, bf16[2,4,384,128]{2,3,0,1:T(8,128)(2,1)}, u32[]{:S(2)}, u32[]{:S(2)}) %collective-permute-start.6) | collective-permute-done | bytes 786464 | tf_op jit(solution)/shard_map/ppermute | solution.py:44
  159.7 6.1 %fusion.14 = (bf16[1,4,4,384,512]{3,4,2,1,0:T(8,128)(2,1)}, bf16[1,4,4,384,512]{3,4,2,1,0:T(8,128)(2,1)}) fusion(bf16[2,4,4,384,256]{3,4,2,1,0:T(8,128)(2,1)S(1)} %maximum_bitcast_fusion, bf16[2,1,4,384,256]{3,4,0,2,1:T(8,128)(2,1)S(1)} %bitcast.156, bf16[2,1,4,384,256]{3,4,0,2,1:T(8,128)(2,1)S(1)} %maximum_bitcast_fusion.1, ...), kind=kLoop, calls=%fused_computation.26 | loop fusion | flops 34603008 | bytes 25165824 | tf_op jit(solution)/shard_map/concatenate | solution.py:59
  165.8 7.0 %convert_reduce_fusion = (f32[768]{0:T(1024)S(1)}, f32[768]{0:T(1024)S(1)}) fusion(bf16[16,768,384]{2,1,0:T(8,128)(2,1)} %all-gather.5.cloned.1.call-done), kind=kLoop, calls=%fused_computation.3 | loop fusion | flops 18872832 | bytes 9443328 | tf_op jit(solution)/shard_map/reduce_sum | solution.py:87
  172.8 10.1 %fusion.2 = bf16[16,768,384]{2,1,0:T(8,128)(2,1)} fusion(bf16[16,768,384]{2,1,0:T(8,128)(2,1)} %all-gather.5.cloned.1.call-done, f32[768]{0:T(1024)S(1)} %get-tuple-element.35, f32[768]{0:T(1024)S(1)} %get-tuple-element.34), kind=kLoop, calls=%fused_computation.5 | loop fusion | flops 18874368 | bytes 18880512 | tf_op jit(solution)/shard_map/convert_element_type | solution.py:89
  182.9 10.8 %fusion.7 = bf16[4,4,768,384]{3,2,1,0:T(8,128)(2,1)} fusion(s32[]{:T(128)S(6)} %select_n.18, bf16[4,4,768,384]{3,2,1,0:T(8,128)(2,1)} %bitcast.148), kind=kLoop, calls=%fused_computation.19 | loop fusion | flops 4718592 | bytes 18874372 | tf_op jit(solution)/shard_map/concatenate | solution.py:68
  193.8 10.1 %bitcast_reduce_fusion.1 = (f32[96,8,4]{1,0,2:T(8,128)S(1)}, f32[96,8,4,128,1,1]{3,1,5,0,2,4:T(8,128)S(1)}) fusion(bf16[4,128,4,4,384,1]{4,1,0,3,2,5:T(8,128)(2,1)} %bitcast.152, s32[]{:T(128)S(6)} %select_n.20, bf16[4,4,768,384]{3,2,1,0:T(8,128)(2,1)} %fusion.7), kind=kOutput, calls=%fused_computation.50 | convolution fusion | flops 4836946944 | bytes 17313796 | tf_op jit(solution)/shard_map/abtr,abrc->tc/dot_general | solution.py:78
  206.3 10.3 %bitcast_reduce_fusion = (f32[96,8,4]{1,0,2:T(8,128)S(1)}, f32[96,8,4,128,1,1]{3,1,5,0,2,4:T(8,128)S(1)}) fusion(bf16[4,128,4,4,384,1]{4,1,0,3,2,5:T(8,128)(2,1)} %bitcast.151, s32[]{:T(128)S(6)} %select_n.20, bf16[4,4,768,384]{3,2,1,0:T(8,128)(2,1)} %fusion.7), kind=kOutput, calls=%fused_computation.43 | convolution fusion | flops 4836946944 | bytes 17313796 | tf_op jit(solution)/shard_map/abtr,abrc->tc/dot_general | solution.py:78
  219.1 9.5 %bitcast_convert_fusion = bf16[768,512]{1,0:T(8,128)(2,1)S(1)} fusion(bf16[4,4,768,384]{3,2,1,0:T(8,128)(2,1)} %bitcast.149, bf16[4,4,384,512]{3,2,1,0:T(8,128)(2,1)} %bitcast.173), kind=kOutput, calls=%fused_computation.42 | convolution fusion | flops 4832231424 | bytes 16515072 | tf_op jit(solution)/shard_map/abtr,abrc->tc/dot_general | solution.py:78
  229.8 32.9 %all_to_all.33 = bf16[96,3,32,128]{3,0,1,2:T(8,128)(2,1)S(1)} all-to-all(bf16[96,3,32,128]{3,0,1,2:T(8,128)(2,1)S(1)} %copy.142), channel_id=1, replica_groups=mesh['tok'=16,'wid'=8] {'tok'}, dimensions={2} | all-to-all | bytes 4718592 | tf_op jit(solution)/shard_map/all_to_all | solution.py:103
  262.9 5.8 %fusion.43 = f32[2,1536]{1,0:T(2,128)S(1)} fusion(bf16[1536,3,2,128]{3,0,2,1:T(8,128)(2,1)S(1)} %bitcast.161), kind=kOutput, calls=%fused_computation.78 | convolution fusion | flops 1222116864 | bytes 1585152 | tf_op jit(solution)/shard_map/while/body/eval_jaxpr/sub | solution.py:115
  268.7 8.3 %fusion.20 = bf16[1536,2,128]{0,2,1:T(8,128)(2,1)S(1)} fusion(f32[2,1536]{1,0:T(2,128)S(1)} %fusion.43, bf16[1536,3,2,128]{3,0,2,1:T(8,128)(2,1)S(1)} %bitcast.162), kind=kOutput, calls=%fused_computation.35 | convolution fusion | flops 2435191296 | bytes 3158016 | tf_op jit(solution)/shard_map/while/body/eval_jaxpr/iqk,kid->qid/dot_general | solution.py:117
  277.7 14.2 %all_to_all.34 = bf16[1536,2,128]{2,1,0:T(2,128)(2,1)S(1)} all-to-all(bf16[1536,2,128]{2,1,0:T(2,128)(2,1)S(1)} %copy.146), channel_id=1, replica_groups=mesh['tok'=16,'wid'=8] {'tok'}, dimensions={0} | all-to-all | bytes 1572864 | tf_op jit(solution)/shard_map/all_to_all | solution.py:122
  294.0 45.7 %all-gather.9.cloned.1.call-done = bf16[96,8,4096]{2,1,0:T(8,128)(2,1)} async-done(((bf16[96,8,512]{2,1,0:T(8,128)(2,1)}), bf16[96,8,4096]{2,1,0:T(8,128)(2,1)}) %all-gather.9.cloned.1.call-update) | async-done | bytes 6291472 | tf_op jit(solution)/shard_map/all_gather | solution.py:124
  339.7 9.8 %add_convert_fusion = bf16[96,8,768]{2,1,0:T(8,128)(2,1)} fusion(bf16[96,8,768]{2,1,0:T(8,128)(2,1)S(1)} %copy-done.6, bf16[96,8,4096]{2,1,0:T(8,128)(2,1)} %all-gather.9.cloned.1.call-done, bf16[4096,768]{1,0:T(8,128)(2,1)} %all-gather.11.cloned.1.call-done), kind=kOutput, calls=%fused_computation.37 | convolution fusion | flops 4833607680 | bytes 14942208 | tf_op jit(solution)/shard_map/dot_general | solution.py:20
  (100 shorter events, 37.2 us)
Async XLA Ops:
  6.5 159.3 %all-gather.5.cloned.1.call-start = ((), (), s32[]{:S(2)}) async-start(), calls=%async_computation.2 | async-start | bytes 10616832 | tf_op jit(solution)/shard_map/all_gather | solution.py:86
  10.6 208.5 %all-gather.7.cloned.1.call-start = ((), (), s32[]{:S(2)}) async-start(), calls=%async_computation.3 | async-start | bytes 6684672 | tf_op jit(solution)/shard_map/all_gather | solution.py:96
  11.3 282.6 %all-gather.11.cloned.1.call-start = ((), (), s32[]{:S(2)}) async-start(), calls=%async_computation.5 | async-start | bytes 6684672 | tf_op jit(solution)/shard_map/all_gather | solution.py:125
  11.9 11.8 %collective-permute-start.9 = (bf16[2,384,256]{1,2,0:T(8,128)(2,1)S(1)}, bf16[2,384,256]{1,2,0:T(8,128)(2,1)S(1)}, u32[]{:S(2)}, u32[]{:S(2)}) collective-permute-start(bf16[2,384,256]{1,2,0:T(8,128)(2,1)S(1)} %get-tuple-element.29), channel_id=1, source_target_pairs={{0,32},{8,40},{16,48},{24,56},{32,64},{40,72},{48,80},{56,88},{64,... | collective-permute-start | bytes 1179656 | tf_op jit(solution)/shard_map/ppermute | solution.py:41
  14.0 10.1 %collective-permute-start.8 = (bf16[2,384,256]{1,2,0:T(8,128)(2,1)S(1)}, bf16[2,384,256]{1,2,0:T(8,128)(2,1)S(1)}, u32[]{:S(2)}, u32[]{:S(2)}) collective-permute-start(bf16[2,384,256]{1,2,0:T(8,128)(2,1)S(1)} %get-tuple-element.29), channel_id=1, source_target_pairs={{0,96},{8,104},{16,112},{24,120},{32,0},{40,8},{48,16},{56,24},{64... | collective-permute-start | bytes 1179656 | tf_op jit(solution)/shard_map/ppermute | solution.py:42
  23.8 6.2 %collective-permute-start.10 = (bf16[2,384,128]{1,2,0:T(8,128)(2,1)S(1)}, bf16[2,384,128]{1,2,0:T(8,128)(2,1)S(1)}, u32[]{:S(2)}, u32[]{:S(2)}) collective-permute-start(bf16[2,384,128]{1,2,0:T(8,128)(2,1)S(1)} %slice.68), channel_id=1, source_target_pairs={{0,32},{8,40},{16,48},{24,56},{32,64},{40,72},{48,80},{56,88},{64,... | collective-permute-start | bytes 589832 | tf_op jit(solution)/shard_map/ppermute | solution.py:44
  24.2 5.9 %collective-permute-start.11 = (bf16[2,384,128]{1,2,0:T(8,128)(2,1)S(1)}, bf16[2,384,128]{1,2,0:T(8,128)(2,1)S(1)}, u32[]{:S(2)}, u32[]{:S(2)}) collective-permute-start(bf16[2,384,128]{1,2,0:T(8,128)(2,1)S(1)} %slice.69), channel_id=1, source_target_pairs={{0,96},{8,104},{16,112},{24,120},{32,0},{40,8},{48,16},{56,24},{64... | collective-permute-start | bytes 589832 | tf_op jit(solution)/shard_map/ppermute | solution.py:45
  26.6 10.5 %collective-permute-start.1 = (bf16[2,384,256]{1,2,0:T(8,128)(2,1)S(1)}, bf16[2,384,256]{1,2,0:T(8,128)(2,1)S(1)}, u32[]{:S(2)}, u32[]{:S(2)}) collective-permute-start(bf16[2,384,256]{1,2,0:T(8,128)(2,1)S(1)} %get-tuple-element.28), channel_id=1, source_target_pairs={{0,8},{8,16},{16,24},{24,0},{32,40},{40,48},{48,56},{56,32},{64,72... | collective-permute-start | bytes 1179656 | tf_op jit(solution)/shard_map/ppermute | solution.py:41
  28.2 9.0 %collective-permute-start = (bf16[2,384,256]{1,2,0:T(8,128)(2,1)S(1)}, bf16[2,384,256]{1,2,0:T(8,128)(2,1)S(1)}, u32[]{:S(2)}, u32[]{:S(2)}) collective-permute-start(bf16[2,384,256]{1,2,0:T(8,128)(2,1)S(1)} %get-tuple-element.28), channel_id=1, source_target_pairs={{0,24},{8,0},{16,8},{24,16},{32,56},{40,32},{48,40},{56,48},{64,88... | collective-permute-start | bytes 1179656 | tf_op jit(solution)/shard_map/ppermute | solution.py:42
  30.4 47.7 %collective-permute-start.13 = (bf16[2,4,384,256]{2,3,1,0:T(8,128)(2,1)S(1)}, bf16[2,4,384,256]{2,3,1,0:T(8,128)(2,1)S(1)}, u32[]{:S(2)}, u32[]{:S(2)}) collective-permute-start(bf16[2,4,384,256]{2,3,1,0:T(8,128)(2,1)S(1)} %get-tuple-element.27), channel_id=1, source_target_pairs={{0,8},{8,16},{16,24},{24,0},{32,40},{40,48},{48,56},{56,32},{64,72... | collective-permute-start | bytes 4718600 | tf_op jit(solution)/shard_map/ppermute | solution.py:41
  32.1 48.8 %collective-permute-start.12 = (bf16[2,4,384,256]{2,3,1,0:T(8,128)(2,1)S(1)}, bf16[2,4,384,256]{2,3,1,0:T(8,128)(2,1)S(1)}, u32[]{:S(2)}, u32[]{:S(2)}) collective-permute-start(bf16[2,4,384,256]{2,3,1,0:T(8,128)(2,1)S(1)} %get-tuple-element.27), channel_id=1, source_target_pairs={{0,24},{8,0},{16,8},{24,16},{32,56},{40,32},{48,40},{56,48},{64,88... | collective-permute-start | bytes 4718600 | tf_op jit(solution)/shard_map/ppermute | solution.py:42
  37.1 37.8 %collective-permute-start.2 = (bf16[2,384,128]{1,2,0:T(8,128)(2,1)S(1)}, bf16[2,384,128]{1,2,0:T(8,128)(2,1)S(1)}, u32[]{:S(2)}, u32[]{:S(2)}) collective-permute-start(bf16[2,384,128]{1,2,0:T(8,128)(2,1)S(1)} %slice.64), channel_id=1, source_target_pairs={{0,8},{8,16},{16,24},{24,0},{32,40},{40,48},{48,56},{56,32},{64,72... | collective-permute-start | bytes 589832 | tf_op jit(solution)/shard_map/ppermute | solution.py:44
  37.3 37.7 %collective-permute-start.3 = (bf16[2,384,128]{1,2,0:T(8,128)(2,1)S(1)}, bf16[2,384,128]{1,2,0:T(8,128)(2,1)S(1)}, u32[]{:S(2)}, u32[]{:S(2)}) collective-permute-start(bf16[2,384,128]{1,2,0:T(8,128)(2,1)S(1)} %slice.65), channel_id=1, source_target_pairs={{0,24},{8,0},{16,8},{24,16},{32,56},{40,32},{48,40},{56,48},{64,88... | collective-permute-start | bytes 589832 | tf_op jit(solution)/shard_map/ppermute | solution.py:45
  75.3 47.9 %collective-permute-start.5 = (bf16[2,4,384,256]{2,3,0,1:T(8,128)(2,1)S(1)}, bf16[2,4,384,256]{2,3,0,1:T(8,128)(2,1)S(1)}, u32[]{:S(2)}, u32[]{:S(2)}) collective-permute-start(bf16[2,4,384,256]{2,3,0,1:T(8,128)(2,1)S(1)} %get-tuple-element.25), channel_id=1, source_target_pairs={{0,32},{8,40},{16,48},{24,56},{32,64},{40,72},{48,80},{56,88},{64,... | collective-permute-start | bytes 4718600 | tf_op jit(solution)/shard_map/ppermute | solution.py:41
  75.4 49.9 %collective-permute-start.4 = (bf16[2,4,384,256]{2,3,0,1:T(8,128)(2,1)S(1)}, bf16[2,4,384,256]{2,3,0,1:T(8,128)(2,1)S(1)}, u32[]{:S(2)}, u32[]{:S(2)}) collective-permute-start(bf16[2,4,384,256]{2,3,0,1:T(8,128)(2,1)S(1)} %get-tuple-element.25), channel_id=1, source_target_pairs={{0,96},{8,104},{16,112},{24,120},{32,0},{40,8},{48,16},{56,24},{64... | collective-permute-start | bytes 4718600 | tf_op jit(solution)/shard_map/ppermute | solution.py:42
  80.2 50.8 %collective-permute-start.14 = (bf16[2,4,384,128]{2,3,1,0:T(8,128)(2,1)}, bf16[2,4,384,128]{2,3,1,0:T(8,128)(2,1)}, u32[]{:S(2)}, u32[]{:S(2)}) collective-permute-start(bf16[2,4,384,128]{2,3,1,0:T(8,128)(2,1)} %slice.70), channel_id=1, source_target_pairs={{0,8},{8,16},{16,24},{24,0},{32,40},{40,48},{48,56},{56,32},{64,72... | collective-permute-start | bytes 2359304 | tf_op jit(solution)/shard_map/ppermute | solution.py:44
  83.2 47.8 %collective-permute-start.15 = (bf16[2,4,384,128]{2,3,1,0:T(8,128)(2,1)}, bf16[2,4,384,128]{2,3,1,0:T(8,128)(2,1)}, u32[]{:S(2)}, u32[]{:S(2)}) collective-permute-start(bf16[2,4,384,128]{2,3,1,0:T(8,128)(2,1)} %slice.71), channel_id=1, source_target_pairs={{0,24},{8,0},{16,8},{24,16},{32,56},{40,32},{48,40},{56,48},{64,88... | collective-permute-start | bytes 2359304 | tf_op jit(solution)/shard_map/ppermute | solution.py:45
  125.3 32.8 %collective-permute-start.6 = (bf16[2,4,384,128]{2,3,0,1:T(8,128)(2,1)}, bf16[2,4,384,128]{2,3,0,1:T(8,128)(2,1)}, u32[]{:S(2)}, u32[]{:S(2)}) collective-permute-start(bf16[2,4,384,128]{2,3,0,1:T(8,128)(2,1)} %slice.66), channel_id=1, source_target_pairs={{0,32},{8,40},{16,48},{24,56},{32,64},{40,72},{48,80},{56,88},{64,... | collective-permute-start | bytes 2359304 | tf_op jit(solution)/shard_map/ppermute | solution.py:44
  127.5 30.7 %collective-permute-start.7 = (bf16[2,4,384,128]{2,3,0,1:T(8,128)(2,1)}, bf16[2,4,384,128]{2,3,0,1:T(8,128)(2,1)}, u32[]{:S(2)}, u32[]{:S(2)}) collective-permute-start(bf16[2,4,384,128]{2,3,0,1:T(8,128)(2,1)} %slice.67), channel_id=1, source_target_pairs={{0,96},{8,104},{16,112},{24,120},{32,0},{40,8},{48,16},{56,24},{64... | collective-permute-start | bytes 2359304 | tf_op jit(solution)/shard_map/ppermute | solution.py:45
  130.9 208.8 %all-gather.9.cloned.1.call-start = ((), (), s32[]{:S(2)}) async-start(), calls=%async_computation.4 | async-start | bytes 7077888 | tf_op jit(solution)/shard_map/all_gather | solution.py:124
  132.5 27.1 %copy-start.3 = (bf16[2,4,384,256]{2,3,0,1:T(8,128)(2,1)S(1)}, bf16[2,4,384,256]{2,3,0,1:T(8,128)(2,1)}, u32[]{:S(2)}) copy-start(bf16[2,4,384,256]{2,3,0,1:T(8,128)(2,1)} %copy-done.2) | copy-start | bytes 4718596
  132.5 27.1 %copy-start.5 = (bf16[2,4,384,256]{2,3,0,1:T(8,128)(2,1)S(1)}, bf16[2,4,384,256]{2,3,0,1:T(8,128)(2,1)}, u32[]{:S(2)}) copy-start(bf16[2,4,384,256]{2,3,0,1:T(8,128)(2,1)} %copy-done.4) | copy-start | bytes 4718596
  206.3 11.5 %copy-start.10 = (f32[512]{0:T(512)S(1)}, f32[512]{0:T(512)}, u32[]{:S(2)}) copy-start(f32[512]{0:T(512)} %param.12) | copy-start | bytes 6148
  277.0 62.7 %copy-start.6 = (bf16[96,8,768]{2,1,0:T(8,128)(2,1)S(1)}, bf16[96,8,768]{2,1,0:T(8,128)(2,1)}, u32[]{:S(2)}) copy-start(bf16[96,8,768]{2,1,0:T(8,128)(2,1)} %param.7) | copy-start | bytes 3538948
  (7 other events, 25.8 us)
Sparse Core Ops, SparseCore 0:
  10.7 57.8 all-gather.4
  70.8 84.6 all-gather.6
  157.7 60.3 all-gather.10
  294.1 45.5 all-gather.8
